TPU v7x, 128 devices: a whole 4x4x4 slice. The times are simulated.
128 devices in a mesh: row: 8 (over z, core), col: 8 (over y_lo, x), dep: 2 (over y_hi).
Axes of the slice: x: 4, y: 4 (y_hi: 2, y_lo: 2; y = y_hi * 2 + y_lo), z: 4, core: 2. Of those that a mesh axis runs over, the one named last changes fastest.
Arguments:
- tokens: bfloat16 [2048, 8192], P(('dep', 'col'), 'row'), may hold values from -6 to 6
- gate_weight: bfloat16 [8192, 14336], P('row', 'col'), may hold values from -0.0625 to 0.0625
- up_weight: bfloat16 [8192, 14336], P('row', 'col'), may hold values from -0.0625 to 0.0625
- cotangent: bfloat16 [2048, 14336], P(('dep', 'row'), 'col'), may hold values from -6 to 6
Outputs:
- hidden: bfloat16 [2048, 14336], P(('dep', 'row'), 'col')
- grad_tokens: bfloat16 [2048, 8192], P(('dep', 'col'), 'row')
- grad_gate_weight: bfloat16 [8192, 14336], P('row', ('col', 'dep'))
- grad_up_weight: bfloat16 [8192, 14336], P('row', ('col', 'dep'))
All inputs are finite; a program needn't handle non-finite values.
Results may differ from a plain program's by a relative error of at most 0.02.
Values may be sent and summed in bfloat16 or wider, within the bound.
No kernel may reach another device: no remote copies, remote signals or barrier semaphores. Data moves between devices by JAX's collectives and lax.ppermute only.
A program may use at most 128 MiB of HBM per device.

v0:
```python
import jax
import jax.numpy as jnp
from jax import lax
from jax.sharding import PartitionSpec as P


def halves(x, dep, half):
    own = lax.dynamic_slice_in_dim(x, dep * half, half, axis=1)
    other = lax.dynamic_slice_in_dim(x, (1 - dep) * half, half, axis=1)
    return (own, other)


def on_device(tokens, gate_weight, up_weight, cotangent):
    width = gate_weight.shape[1]
    half = width // 2
    dep = lax.axis_index("dep")
    n_col = lax.axis_size("col")
    contract = (((0,), (0,)), ((), ()))
    transposed = (((1,), (1,)), ((), ()))
    pair = [(0, 1), (1, 0)]

    def gather_col(block):
        return lax.all_to_all(jnp.tile(block, (n_col, 1)), "col", 0, 0, tiled=True)

    partner_tokens = lax.ppermute(tokens, "dep", pair)
    gathered = gather_col(tokens)
    first = jnp.dot(gathered, gate_weight, preferred_element_type=jnp.float32)
    second = jnp.dot(gathered, up_weight, preferred_element_type=jnp.float32)
    joined = lax.psum_scatter(
        jnp.concatenate([first, second], axis=1).astype(jnp.bfloat16),
        "row",
        scatter_dimension=0,
        tiled=True,
    )
    gathered_partner = gather_col(partner_tokens)
    joined, gathered_partner = lax.optimization_barrier((joined, gathered_partner))
    gate = joined[:, :width]
    up = joined[:, width:]
    upstream = cotangent

    def grads(gate, up, upstream):
        gate, up, upstream = (x.astype(jnp.float32) for x in (gate, up, upstream))
        sigma = jax.nn.sigmoid(gate)
        active = gate * sigma
        grad_gate = (upstream * up * sigma * (1.0 + gate * (1.0 - sigma))).astype(jnp.bfloat16)
        return (grad_gate, (upstream * active).astype(jnp.bfloat16))

    gate_own, gate_other = halves(gate, dep, half)
    up_own, up_other = halves(up, dep, half)
    up_stream_own, up_stream_other = halves(upstream, dep, half)
    grad_gate_other, grad_up_other = grads(gate_other, up_other, up_stream_other)
    payload = jnp.concatenate([grad_gate_other, grad_up_other], axis=1)
    payload, gate_own, up_own, up_stream_own, gate, up = lax.optimization_barrier(
        (payload, gate_own, up_own, up_stream_own, gate, up)
    )
    partner_gate, partner_up = jnp.split(lax.ppermute(payload, "dep", pair), 2, axis=1)
    grad_gate_own, grad_up_own = grads(gate_own, up_own, up_stream_own)
    gate, up = (gate.astype(jnp.float32), up.astype(jnp.float32))
    hidden = (gate * jax.nn.sigmoid(gate) * up).astype(jnp.bfloat16)
    gate_own, up_own, gate_other, up_other = (
        grad_gate_own,
        grad_up_own,
        grad_gate_other,
        grad_up_other,
    )
    full = lax.all_gather(
        jnp.concatenate([gate_own, up_own, gate_other, up_other, partner_gate, partner_up], axis=1),
        "row",
        axis=0,
        tiled=True,
    )
    wg_own, wg_other = halves(gate_weight, dep, half)
    wu_own, wu_other = halves(up_weight, dep, half)
    weights = jnp.concatenate([wg_own, wu_own, wg_other, wu_other], axis=1)
    term = lax.dot_general(
        full[:, : 2 * width], weights, transposed, preferred_element_type=jnp.float32
    )
    term = term.astype(jnp.bfloat16).reshape(n_col, -1, term.shape[1])
    term, gathered, gathered_partner = lax.optimization_barrier((term, gathered, gathered_partner))
    parts = lax.all_to_all(term, "col", 0, 0, tiled=True)
    grad_tokens = parts.astype(jnp.float32).sum(axis=0).astype(jnp.bfloat16)

    def weight_grad(own, partner):
        mine = lax.dot_general(gathered, own, contract, preferred_element_type=jnp.float32)
        theirs = lax.dot_general(
            gathered_partner, partner, contract, preferred_element_type=jnp.float32
        )
        return (
            mine.astype(jnp.bfloat16).astype(jnp.float32)
            + theirs.astype(jnp.bfloat16).astype(jnp.float32)
        ).astype(jnp.bfloat16)

    sum_gate = weight_grad(full[:, :half], full[:, 2 * width : 2 * width + half])
    sum_up = weight_grad(full[:, half:width], full[:, 2 * width + half :])
    return (hidden, grad_tokens, sum_gate, sum_up)


def solution(mesh):
    return jax.shard_map(
        on_device,
        mesh=mesh,
        in_specs=(
            P(("dep", "col"), "row"),
            P("row", "col"),
            P("row", "col"),
            P(("dep", "row"), "col"),
        ),
        out_specs=(
            P(("dep", "row"), "col"),
            P(("dep", "col"), "row"),
            P("row", ("col", "dep")),
            P("row", ("col", "dep")),
        ),
        check_vma=False,
    )
```

profile of v0, /device:TPU:6, one launch (start us, length us, event | category | flops | bytes accessed | tf_op | source)
XLA Modules:
  0.0 237.5 jit_solution(15468545211119573866)
XLA Ops:
  7.2 0.0 reduce-scatter.2.cloned.1.call-start
  7.2 1.2 tile.4
  8.4 0.0 copy-start
  8.4 30.9 %all_to_all.23 = bf16[8,128,1024]{2,1,0:T(8,128)(2,1)S(1)} all-to-all(bf16[8,128,1024]{2,1,0:T(8,128)(2,1)S(1)} %tile.4), channel_id=1, replica_groups=mesh['row'=8,'col'=8,'dep'=2] {'col'}, dimensions={0} | all-to-all | bytes 4194304 | tf_op jit(solution)/shard_map/all_to_all | solution.py:23
  39.4 0.0 copy-start.2
  39.4 0.0 copy-done
  39.4 0.0 copy-start.1
  39.4 4.2 %convolution_convert_fusion = bf16[1024,1792]{1,0:T(8,128)(2,1)S(1)} fusion(bf16[1024,1024]{1,0:T(8,128)(2,1)S(1)} %bitcast.11, bf16[1024,1792]{1,0:T(8,128)(2,1)S(1)} %copy-done), kind=kOutput, calls=%fused_computation.10 | convolution fusion | flops 3759931392 | bytes 9437184 | tf_op jit(solution)/shard_map/dot_general | solution.py:28
  43.5 0.0 copy-done.2
  43.5 0.0 copy-done.1
  43.5 5.4 %convolution_convert_fusion.1 = bf16[1024,1792]{1,0:T(8,128)(2,1)} fusion(bf16[1024,1024]{1,0:T(8,128)(2,1)S(1)} %bitcast.12, bf16[1024,1792]{1,0:T(8,128)(2,1)S(1)} %copy-done.1), kind=kOutput, calls=%fused_computation.11 | convolution fusion | flops 3759931392 | bytes 9437184 | tf_op jit(solution)/shard_map/dot_general | solution.py:27
  48.9 5.5 %pad_maximum_fusion = bf16[1024,3584]{1,0:T(8,128)(2,1)} fusion(bf16[1024,1792]{1,0:T(8,128)(2,1)S(1)} %convolution_convert_fusion, bf16[1024,1792]{1,0:T(8,128)(2,1)} %convolution_convert_fusion.1), kind=kLoop, calls=%fused_computation.2 | loop fusion | flops 14680064 | bytes 14680064 | tf_op jit(solution)/shard_map/concatenate | solution.py:30
  54.5 0.0 copy-start.7
  54.5 0.0 reduce-scatter.2.cloned.1.call-update
  54.5 0.9 copy-done.7
  55.4 2.9 %collective-permute-start = (bf16[128,1024]{1,0:T(8,128)(2,1)S(1)}, bf16[128,1024]{1,0:T(8,128)(2,1)S(1)}, u32[]{:S(2)}, u32[]{:S(2)}) collective-permute-start(bf16[128,1024]{1,0:T(8,128)(2,1)S(1)} %copy-done.7), channel_id=1, source_target_pairs={{0,1},{1,0},{2,3},{3,2},{4,5},{5,4},{6,7},{7,6},{8,9},{9,8},{10,11... | collective-permute-start | bytes 786440 | tf_op jit(solution)/shard_map/ppermute | solution.py:25
  58.3 5.2 %collective-permute-done = bf16[128,1024]{1,0:T(8,128)(2,1)S(1)} collective-permute-done((bf16[128,1024]{1,0:T(8,128)(2,1)S(1)}, bf16[128,1024]{1,0:T(8,128)(2,1)S(1)}, u32[]{:S(2)}, u32[]{:S(2)}) %collective-permute-start) | collective-permute-done | bytes 262176 | tf_op jit(solution)/shard_map/ppermute | solution.py:25
  63.5 1.6 tile.5
  65.1 5.9 %all-to-all-start.1 = ((bf16[8,128,1024]{2,1,0:T(8,128)(2,1)}), bf16[8,128,1024]{2,1,0:T(8,128)(2,1)S(1)}, u32[]{:S(2)}, u32[]{:S(2)}) async-start(bf16[8,128,1024]{2,1,0:T(8,128)(2,1)} %tile.5), calls=%async_computation.2 | async-start | bytes 4194304 | tf_op jit(solution)/shard_map/all_to_all | solution.py:23
  71.1 0.0 all-gather.2.cloned.1.call-start
  71.1 0.0 copy-done.6
  71.1 22.6 %all-to-all-done.1 = bf16[8,128,1024]{2,1,0:T(8,128)(2,1)S(1)} async-done(((bf16[8,128,1024]{2,1,0:T(8,128)(2,1)}), bf16[8,128,1024]{2,1,0:T(8,128)(2,1)S(1)}, u32[]{:S(2)}, u32[]{:S(2)}) %all-to-all-start.1) | async-done | bytes 2097184 | tf_op jit(solution)/shard_map/all_to_all | solution.py:23
  93.7 10.4 %reduce-scatter.2.cloned.1.call-done = bf16[128,3584]{1,0:T(8,128)(2,1)} async-done(((bf16[1024,3584]{1,0:T(8,128)(2,1)}), bf16[128,3584]{1,0:T(8,128)(2,1)}) %reduce-scatter.2.cloned.1.call-update) | async-done | bytes 917520 | tf_op jit(solution)/shard_map/reduce_scatter | solution.py:29
  104.1 0.0 copy-done.4
  104.1 1.2 fusion.50
  105.4 0.3 fusion.33
  105.7 3.1 %collective-permute-start.1 = (bf16[128,1792]{1,0:T(8,128)(2,1)S(1)}, bf16[128,1792]{1,0:T(8,128)(2,1)S(1)}, u32[]{:S(2)}, u32[]{:S(2)}) collective-permute-start(bf16[128,1792]{1,0:T(8,128)(2,1)S(1)} %pad_maximum_fusion.1), channel_id=1, source_target_pairs={{0,1},{1,0},{2,3},{3,2},{4,5},{5,4},{6,7},{7,6},{8,9},{9,8},{10,11... | collective-permute-start | bytes 1376264 | tf_op jit(solution)/shard_map/ppermute | solution.py:56
  108.8 0.9 fusion.48
  109.7 0.8 fusion.47
  110.6 0.7 constant_dynamic-update-slice_fusion.2
  111.3 0.7 constant_dynamic-update-slice_fusion.1
  112.0 6.8 %collective-permute-done.1 = bf16[128,1792]{1,0:T(8,128)(2,1)S(1)} collective-permute-done((bf16[128,1792]{1,0:T(8,128)(2,1)S(1)}, bf16[128,1792]{1,0:T(8,128)(2,1)S(1)}, u32[]{:S(2)}, u32[]{:S(2)}) %collective-permute-start.1) | collective-permute-done | bytes 458784 | tf_op jit(solution)/shard_map/ppermute | solution.py:56
  118.9 0.8 constant_dynamic-update-slice_fusion
  119.7 0.0 all-gather.2.cloned.1.call-update
  119.7 5.8 %constant_dynamic-slice_fusion.1 = (bf16[1024,896]{1,0:T(8,128)(2,1)S(1)}, bf16[1024,896]{1,0:T(8,128)(2,1)}, bf16[1024,896]{1,0:T(8,128)(2,1)}, bf16[1024,896]{1,0:T(8,128)(2,1)}) fusion(bf16[1024,1792]{1,0:T(8,128)(2,1)} %param.6, s32[]{:T(128)S(6)} %select_n.5, s32[]{:T(128)S(6)} %select_n.4, bf16[1024,1792]{1,0:T(8,128)(2,1)} %param.5), kind=kLoop, calls=%fused_computation.63 | loop fusion | bytes 14680072 | tf_op jit(solution)/shard_map/dynamic_slice | solution.py:8
  125.5 1.0 fusion.30
  126.6 54.8 %all-gather.2.cloned.1.call-done = bf16[1024,5376]{1,0:T(8,128)(2,1)} async-done(((bf16[128,5376]{1,0:T(8,128)(2,1)}), bf16[1024,5376]{1,0:T(8,128)(2,1)}) %all-gather.2.cloned.1.call-update) | async-done | bytes 11010064 | tf_op jit(solution)/shard_map/all_gather | solution.py:66
  181.3 12.9 %fusion.9 = bf16[1024,1024]{1,0:T(8,128)(2,1)} fusion(bf16[1024,896]{1,0:T(8,128)(2,1)} %get-tuple-element.29, bf16[1024,896]{1,0:T(8,128)(2,1)} %get-tuple-element.36, bf16[1024,896]{1,0:T(8,128)(2,1)S(1)} %get-tuple-element.28, bf16[1024,896]{1,0:T(8,128)(2,1)} %get-tuple-element.37, bf16[1024,5376]{1,0:T(8,128)(2,1)} %all-gather.2.cloned.1.call-done), kind=kOutput, calls=%fused_computation.14 | convolution fusion | flops 7546601472 | bytes 16777216 | tf_op jit(solution)/shard_map/dot_general | solution.py:75
  194.2 5.7 %all-to-all-start.2 = ((bf16[8,128,1024]{2,1,0:T(8,128)(2,1)}), bf16[8,128,1024]{2,1,0:T(8,128)(2,1)S(1)}, u32[]{:S(2)}, u32[]{:S(2)}) async-start(bf16[8,128,1024]{2,1,0:T(8,128)(2,1)} %bitcast.17), calls=%async_computation.3 | async-start | bytes 4194304 | tf_op jit(solution)/shard_map/all_to_all | solution.py:80
  200.0 4.7 %fusion.16 = bf16[1024,896]{1,0:T(8,128)(2,1)S(1)} fusion(bf16[1024,1024]{1,0:T(8,128)(2,1)} %bitcast.13, bf16[1024,5376]{1,0:T(8,128)(2,1)} %all-gather.2.cloned.1.call-done), kind=kOutput, calls=%fused_computation.17 | convolution fusion | flops 1879048192 | bytes 5767168 | tf_op jit(solution)/shard_map/dot_general | solution.py:84
  204.6 0.0 copy-done.3
  204.7 0.0 copy-start.5
  204.7 4.1 %fusion.20 = bf16[1024,896]{1,0:T(8,128)(2,1)S(1)} fusion(bf16[1024,1024]{1,0:T(8,128)(2,1)S(1)} %bitcast.14, bf16[1024,5376]{1,0:T(8,128)(2,1)} %all-gather.2.cloned.1.call-done), kind=kOutput, calls=%fused_computation.21 | convolution fusion | flops 1879048192 | bytes 5767168 | tf_op jit(solution)/shard_map/dot_general | solution.py:84
  208.7 0.0 copy-done.5
  208.8 5.2 %add_convert_fusion.1 = bf16[1024,896]{1,0:T(8,128)(2,1)} fusion(bf16[1024,896]{1,0:T(8,128)(2,1)S(1)} %fusion.20, bf16[1024,1024]{1,0:T(8,128)(2,1)S(1)} %bitcast.15, bf16[1024,5376]{1,0:T(8,128)(2,1)} %all-gather.2.cloned.1.call-done), kind=kOutput, calls=%fused_computation.13 | convolution fusion | flops 1883635712 | bytes 7602176 | tf_op jit(solution)/shard_map/dot_general | solution.py:85
  214.0 5.2 %add_convert_fusion = bf16[1024,896]{1,0:T(8,128)(2,1)} fusion(bf16[1024,896]{1,0:T(8,128)(2,1)S(1)} %fusion.16, bf16[1024,1024]{1,0:T(8,128)(2,1)S(1)} %bitcast.16, bf16[1024,5376]{1,0:T(8,128)(2,1)} %all-gather.2.cloned.1.call-done), kind=kOutput, calls=%fused_computation.12 | convolution fusion | flops 1883635712 | bytes 7602176 | tf_op jit(solution)/shard_map/dot_general | solution.py:85
  219.2 10.4 %all-to-all-done.2 = bf16[8,128,1024]{2,1,0:T(8,128)(2,1)S(1)} async-done(((bf16[8,128,1024]{2,1,0:T(8,128)(2,1)}), bf16[8,128,1024]{2,1,0:T(8,128)(2,1)S(1)}, u32[]{:S(2)}, u32[]{:S(2)}) %all-to-all-start.2) | async-done | bytes 2097184 | tf_op jit(solution)/shard_map/all_to_all | solution.py:80
  229.6 1.1 reduce_sum.12
  (6 shorter events, 0.1 us)
Async XLA Ops:
  7.2 96.9 %reduce-scatter.2.cloned.1.call-start = ((), (), s32[]{:S(2)}) async-start(), calls=%async_computation.4 | async-start | bytes 8257536 | tf_op jit(solution)/shard_map/reduce_scatter | solution.py:29
  8.4 30.9 %copy-start = (bf16[1024,1792]{1,0:T(8,128)(2,1)S(1)}, bf16[1024,1792]{1,0:T(8,128)(2,1)}, u32[]{:S(2)}) copy-start(bf16[1024,1792]{1,0:T(8,128)(2,1)} %param.6) | copy-start | bytes 11010052
  39.4 4.2 %copy-start.2 = (bf16[8,128,1024]{2,1,0:T(8,128)(2,1)}, bf16[8,128,1024]{2,1,0:T(8,128)(2,1)S(1)}, u32[]{:S(2)}) copy-start(bf16[8,128,1024]{2,1,0:T(8,128)(2,1)S(1)} %all_to_all.23) | copy-start | bytes 6291460
  39.4 4.2 %copy-start.1 = (bf16[1024,1792]{1,0:T(8,128)(2,1)S(1)}, bf16[1024,1792]{1,0:T(8,128)(2,1)}, u32[]{:S(2)}) copy-start(bf16[1024,1792]{1,0:T(8,128)(2,1)} %param.5) | copy-start | bytes 11010052
  54.5 0.9 copy-start.7
  55.4 8.1 %collective-permute-start = (bf16[128,1024]{1,0:T(8,128)(2,1)S(1)}, bf16[128,1024]{1,0:T(8,128)(2,1)S(1)}, u32[]{:S(2)}, u32[]{:S(2)}) collective-permute-start(bf16[128,1024]{1,0:T(8,128)(2,1)S(1)} %copy-done.7), channel_id=1, source_target_pairs={{0,1},{1,0},{2,3},{3,2},{4,5},{5,4},{6,7},{7,6},{8,9},{9,8},{10,11... | collective-permute-start | bytes 786440 | tf_op jit(solution)/shard_map/ppermute | solution.py:25
  65.1 5.9 %copy-start.6 = (bf16[128,1792]{1,0:T(8,128)(2,1)S(1)}, bf16[128,1792]{1,0:T(8,128)(2,1)}, u32[]{:S(2)}) copy-start(bf16[128,1792]{1,0:T(8,128)(2,1)} %param.7) | copy-start | bytes 1376260
  65.1 28.5 %all-to-all-start.1 = ((bf16[8,128,1024]{2,1,0:T(8,128)(2,1)}), bf16[8,128,1024]{2,1,0:T(8,128)(2,1)S(1)}, u32[]{:S(2)}, u32[]{:S(2)}) async-start(bf16[8,128,1024]{2,1,0:T(8,128)(2,1)} %tile.5), calls=%async_computation.2 | async-start | bytes 4194304 | tf_op jit(solution)/shard_map/all_to_all | solution.py:23
  71.1 110.3 %all-gather.2.cloned.1.call-start = ((), (), s32[]{:S(2)}) async-start(), calls=%async_computation.5 | async-start | bytes 12386304 | tf_op jit(solution)/shard_map/all_gather | solution.py:66
  93.7 10.4 %copy-start.4 = (bf16[8,128,1024]{2,1,0:T(8,128)(2,1)}, bf16[8,128,1024]{2,1,0:T(8,128)(2,1)S(1)}, u32[]{:S(2)}) copy-start(bf16[8,128,1024]{2,1,0:T(8,128)(2,1)S(1)} %all-to-all-done.1) | copy-start | bytes 6291460
  105.7 13.2 %collective-permute-start.1 = (bf16[128,1792]{1,0:T(8,128)(2,1)S(1)}, bf16[128,1792]{1,0:T(8,128)(2,1)S(1)}, u32[]{:S(2)}, u32[]{:S(2)}) collective-permute-start(bf16[128,1792]{1,0:T(8,128)(2,1)S(1)} %pad_maximum_fusion.1), channel_id=1, source_target_pairs={{0,1},{1,0},{2,3},{3,2},{4,5},{5,4},{6,7},{7,6},{8,9},{9,8},{10,11... | collective-permute-start | bytes 1376264 | tf_op jit(solution)/shard_map/ppermute | solution.py:56
  194.2 35.3 %all-to-all-start.2 = ((bf16[8,128,1024]{2,1,0:T(8,128)(2,1)}), bf16[8,128,1024]{2,1,0:T(8,128)(2,1)S(1)}, u32[]{:S(2)}, u32[]{:S(2)}) async-start(bf16[8,128,1024]{2,1,0:T(8,128)(2,1)} %bitcast.17), calls=%async_computation.3 | async-start | bytes 4194304 | tf_op jit(solution)/shard_map/all_to_all | solution.py:80
  200.0 4.7 %copy-start.3 = (bf16[8,128,1024]{2,1,0:T(8,128)(2,1)S(1)}, bf16[8,128,1024]{2,1,0:T(8,128)(2,1)}, u32[]{:S(2)}) copy-start(bf16[8,128,1024]{2,1,0:T(8,128)(2,1)} %copy-done.2) | copy-start | bytes 6291460
  204.7 4.1 %copy-start.5 = (bf16[8,128,1024]{2,1,0:T(8,128)(2,1)S(1)}, bf16[8,128,1024]{2,1,0:T(8,128)(2,1)}, u32[]{:S(2)}) copy-start(bf16[8,128,1024]{2,1,0:T(8,128)(2,1)} %copy-done.4) | copy-start | bytes 6291460
Sparse Core Ops, SparseCore 0:
  54.6 49.4 reduce-scatter.1
  119.9 61.4 all-gather.1
where the time goes:
time: 238 us
  waiting for transfers between devices  110 us (46%)
  matrix products  41.6 us (17%)
  blocking collectives  30.9 us (13%)
  starting transfers between devices  17.7 us (7%)
  between operations  14.2 us (6%)
  local copies, waits for them, and re-layouts  13.2 us (6%)
  other arithmetic  9.78 us (4%)
    all_gather x1, waiting for transfers between devices, on_device(): lax.all_gather(jnp.concatenate([gate_own, up_own, gate_other, up_other, p...  54.8 us
    all_to_all x1, blocking collectives, gather_col(): return lax.all_to_all(jnp.tile(block, (n_col, 1)), 'col', 0, 0, tiled=True)  30.9 us
    all_to_all x1, waiting for transfers between devices, gather_col(): return lax.all_to_all(jnp.tile(block, (n_col, 1)), 'col', 0, 0, tiled=True)  22.6 us
    dot_general x1, matrix products, on_device(): lax.dot_general(full[:, :2 * width], weights, transposed, preferred_eleme...  12.9 us
    dot_general x2, matrix products, weight_grad(): lax.dot_general(gathered_partner, partner, contract, preferred_element_ty...  10.4 us
    reduce_scatter x1, waiting for transfers between devices, on_device(): lax.psum_scatter(jnp.concatenate([first, second], axis=1).astype(jnp.bflo...  10.4 us
    all_to_all x1, waiting for transfers between devices, on_device(): parts = lax.all_to_all(term, 'col', 0, 0, tiled=True)  10.4 us
    dot_general x2, matrix products, weight_grad(): lax.dot_general(gathered, own, contract, preferred_element_type=jnp.float32)  8.74 us
  transfers between devices with their start and end apart: 6, of which 6 were waited for; matrix products, arithmetic and copies ran while one was open for 13% of the time, Pallas kernels for 0%

commit v1 on v0

--- a/solution.py
+++ b/solution.py
@@ -11,6 +11,23 @@
 
 
 def on_device(tokens, gate_weight, up_weight, cotangent):
+
+    def series_play(slab_in, shard_axis):
+        many = lax.axis_size(shard_axis)
+        then = map(lambda rr: (rr, (rr + 1) % many), range(many))
+        history = list(then)
+        before = range(many)
+        store = list(map(lambda rr: (rr, (rr - 1) % many), before))
+        e_next, shaped = ([slab_in], [slab_in])
+        for _ in range(many // 2):
+            w1 = lax.ppermute(e_next[-1], shard_axis, history)
+            e_next.append(w1)
+        for _ in range((many - 1) // 2):
+            newest = lax.ppermute(shaped[-1], shard_axis, store)
+            shaped.append(newest)
+        low = jnp.concatenate([*e_next[::-1], *shaped[1:]], 0)
+        return jnp.roll(low, (lax.axis_index(shard_axis) - many // 2) * slab_in.shape[0], 0)
+
     width = gate_weight.shape[1]
     half = width // 2
     dep = lax.axis_index("dep")
@@ -63,11 +80,9 @@
         grad_gate_other,
         grad_up_other,
     )
-    full = lax.all_gather(
+    full = series_play(
         jnp.concatenate([gate_own, up_own, gate_other, up_other, partner_gate, partner_up], axis=1),
         "row",
-        axis=0,
-        tiled=True,
     )
     wg_own, wg_other = halves(gate_weight, dep, half)
     wu_own, wu_other = halves(up_weight, dep, half)

time: 238 us -> 272 us (1.14); the launches traced: 238 us -> 267 us
  local copies, waits for them, and re-layouts: 13.2 us -> 30.9 us
  starting transfers between devices: 17.7 us -> 26.3 us
    ppermute x0 -> x7, waiting for transfers between devices: none -> 62.4 us  [the longest x4 62.4 us: series_play(): w1 = lax.ppermute(e_next[-1], shard_axis, history)]
    all_gather x1 -> x0, waiting for transfers between devices: 54.8 us -> none  [on_device(): lax.all_gather(jnp.concatenate([gate_own, up_own, gate_other, up_other, p...]
    unnamed x18 -> x55, local copies, waits for them, and re-layouts: 2.41 us -> 22.7 us
    all_to_all x1, waiting for transfers between devices: 10.4 us -> 1.14 us  [on_device(): parts = lax.all_to_all(term, 'col', 0, 0, tiled=True)]
    ppermute x0 -> x7, starting transfers between devices: none -> 8.84 us  [the longest x3 8.81 us: series_play(): newest = lax.ppermute(shaped[-1], shard_axis, store)]
  transfers between devices with their start and end apart: 6 -> 12, of which waited for: 6 -> 9; matrix products, arithmetic and copies ran while one was open for 13% -> 12% of each run, Pallas kernels for 0% -> 0%
where the time goes in v1:
time: 272 us; the launch traced here: 267 us
  waiting for transfers between devices  111 us (41%)
  matrix products  41.8 us (15%)
  local copies, waits for them, and re-layouts  30.9 us (11%)
  blocking collectives  30.7 us (11%)
  starting transfers between devices  26.3 us (10%)
  between operations  14.4 us (5%)
  other arithmetic  12.1 us (4%)
    ppermute x4, waiting for transfers between devices, series_play(): w1 = lax.ppermute(e_next[-1], shard_axis, history)  62.4 us
    all_to_all x1, blocking collectives, gather_col(): return lax.all_to_all(jnp.tile(block, (n_col, 1)), 'col', 0, 0, tiled=True)  30.7 us
    unnamed x55, local copies, waits for them, and re-layouts  22.7 us
    all_to_all x1, waiting for transfers between devices, gather_col(): return lax.all_to_all(jnp.tile(block, (n_col, 1)), 'col', 0, 0, tiled=True)  22.6 us
    dot_general x1, matrix products, on_device(): lax.dot_general(full[:, :2 * width], weights, transposed, preferred_eleme...  12.1 us
    reduce_scatter x1, waiting for transfers between devices, on_device(): lax.psum_scatter(jnp.concatenate([first, second], axis=1).astype(jnp.bflo...  10.6 us
    dot_general x2, matrix products, weight_grad(): lax.dot_general(gathered_partner, partner, contract, preferred_element_ty...  10.4 us
    ppermute x1, waiting for transfers between devices, on_device(): lax.ppermute(payload, 'dep', pair)  8.94 us
  transfers between devices with their start and end apart: 12, of which 9 were waited for; matrix products, arithmetic and copies ran while one was open for 12% of the time, Pallas kernels for 0%

profile of v1, /device:TPU:6, one launch (start us, length us, event | category | flops | bytes accessed | tf_op | source)
XLA Modules:
  0.0 267.0 jit_solution(7506856482674438950)
XLA Ops:
  7.2 1.4 tile.4
  8.6 30.7 %all_to_all.23 = bf16[8,128,1024]{2,1,0:T(8,128)(2,1)S(1)} all-to-all(bf16[8,128,1024]{2,1,0:T(8,128)(2,1)S(1)} %tile.4), channel_id=1, replica_groups=mesh['row'=8,'col'=8,'dep'=2] {'col'}, dimensions={0} | all-to-all | bytes 4194304 | tf_op jit(solution)/shard_map/all_to_all | solution.py:40
  39.2 5.4 %convolution_convert_fusion = bf16[1024,1792]{1,0:T(8,128)(2,1)} fusion(bf16[1024,1024]{1,0:T(8,128)(2,1)S(1)} %bitcast.13, bf16[1024,1792]{1,0:T(8,128)(2,1)S(1)} %copy-done.8), kind=kOutput, calls=%fused_computation.10 | convolution fusion | flops 3759931392 | bytes 9437184 | tf_op jit(solution)/shard_map/dot_general | solution.py:45
  44.6 5.4 %convolution_convert_fusion.1 = bf16[1024,1792]{1,0:T(8,128)(2,1)} fusion(bf16[1024,1024]{1,0:T(8,128)(2,1)S(1)} %bitcast.14, bf16[1024,1792]{1,0:T(8,128)(2,1)S(1)} %copy-done.9), kind=kOutput, calls=%fused_computation.11 | convolution fusion | flops 3759931392 | bytes 9437184 | tf_op jit(solution)/shard_map/dot_general | solution.py:44
  50.0 6.6 %pad_maximum_fusion = bf16[1024,3584]{1,0:T(8,128)(2,1)} fusion(bf16[1024,1792]{1,0:T(8,128)(2,1)} %convolution_convert_fusion, bf16[1024,1792]{1,0:T(8,128)(2,1)} %convolution_convert_fusion.1), kind=kLoop, calls=%fused_computation.2 | loop fusion | flops 14680064 | bytes 14680064 | tf_op jit(solution)/shard_map/concatenate | solution.py:47
  56.6 0.9 copy-done.15
  57.6 2.9 %collective-permute-start = (bf16[128,1024]{1,0:T(8,128)(2,1)S(1)}, bf16[128,1024]{1,0:T(8,128)(2,1)S(1)}, u32[]{:S(2)}, u32[]{:S(2)}) collective-permute-start(bf16[128,1024]{1,0:T(8,128)(2,1)S(1)} %copy-done.15), channel_id=1, source_target_pairs={{0,1},{1,0},{2,3},{3,2},{4,5},{5,4},{6,7},{7,6},{8,9},{9,8},{10,11... | collective-permute-start | bytes 786440 | tf_op jit(solution)/shard_map/ppermute | solution.py:42
  60.5 5.2 %collective-permute-done = bf16[128,1024]{1,0:T(8,128)(2,1)S(1)} collective-permute-done((bf16[128,1024]{1,0:T(8,128)(2,1)S(1)}, bf16[128,1024]{1,0:T(8,128)(2,1)S(1)}, u32[]{:S(2)}, u32[]{:S(2)}) %collective-permute-start) | collective-permute-done | bytes 262176 | tf_op jit(solution)/shard_map/ppermute | solution.py:42
  65.6 1.7 tile.5
  67.3 5.8 %all-to-all-start.1 = ((bf16[8,128,1024]{2,1,0:T(8,128)(2,1)}), bf16[8,128,1024]{2,1,0:T(8,128)(2,1)S(1)}, u32[]{:S(2)}, u32[]{:S(2)}) async-start(bf16[8,128,1024]{2,1,0:T(8,128)(2,1)} %tile.5), calls=%async_computation.2 | async-start | bytes 4194304 | tf_op jit(solution)/shard_map/all_to_all | solution.py:40
  73.1 22.6 %all-to-all-done.1 = bf16[8,128,1024]{2,1,0:T(8,128)(2,1)S(1)} async-done(((bf16[8,128,1024]{2,1,0:T(8,128)(2,1)}), bf16[8,128,1024]{2,1,0:T(8,128)(2,1)S(1)}, u32[]{:S(2)}, u32[]{:S(2)}) %all-to-all-start.1) | async-done | bytes 2097184 | tf_op jit(solution)/shard_map/all_to_all | solution.py:40
  95.7 10.6 %reduce-scatter.2.cloned.1.call-done = bf16[128,3584]{1,0:T(8,128)(2,1)} async-done(((bf16[1024,3584]{1,0:T(8,128)(2,1)}), bf16[128,3584]{1,0:T(8,128)(2,1)}) %reduce-scatter.2.cloned.1.call-update) | async-done | bytes 917520 | tf_op jit(solution)/shard_map/reduce_scatter | solution.py:46
  106.2 1.2 fusion.51
  107.5 0.3 fusion.33
  107.8 3.1 %collective-permute-start.1 = (bf16[128,1792]{1,0:T(8,128)(2,1)S(1)}, bf16[128,1792]{1,0:T(8,128)(2,1)S(1)}, u32[]{:S(2)}, u32[]{:S(2)}) collective-permute-start(bf16[128,1792]{1,0:T(8,128)(2,1)S(1)} %pad_maximum_fusion.1), channel_id=1, source_target_pairs={{0,1},{1,0},{2,3},{3,2},{4,5},{5,4},{6,7},{7,6},{8,9},{9,8},{10,11... | collective-permute-start | bytes 1376264 | tf_op jit(solution)/shard_map/ppermute | solution.py:73
  110.9 0.9 constant_dynamic-update-slice_fusion.4
  111.8 0.2 constant_dynamic-update-slice_fusion.3
  112.1 8.9 %collective-permute-done.1 = bf16[128,1792]{1,0:T(8,128)(2,1)S(1)} collective-permute-done((bf16[128,1792]{1,0:T(8,128)(2,1)S(1)}, bf16[128,1792]{1,0:T(8,128)(2,1)S(1)}, u32[]{:S(2)}, u32[]{:S(2)}) %collective-permute-start.1) | collective-permute-done | bytes 458784 | tf_op jit(solution)/shard_map/ppermute | solution.py:73
  121.1 18.9 %collective-permute-done.2 = bf16[128,5376]{1,0:T(8,128)(2,1)S(1)} collective-permute-done((bf16[128,5376]{1,0:T(8,128)(2,1)S(1)}, bf16[128,5376]{1,0:T(8,128)(2,1)S(1)}, u32[]{:S(2)}, u32[]{:S(2)}) %collective-permute-start.2) | collective-permute-done | bytes 1376288 | tf_op jit(solution)/shard_map/ppermute | solution.py:23
  140.0 1.1 copy-done
  141.1 3.0 %collective-permute-start.6 = (bf16[128,5376]{1,0:T(8,128)(2,1)S(1)}, bf16[128,5376]{1,0:T(8,128)(2,1)}, u32[]{:S(2)}, u32[]{:S(2)}) collective-permute-start(bf16[128,5376]{1,0:T(8,128)(2,1)S(1)} %constant_dynamic-update-slice_fusion), channel_id=1, source_target_pairs={{0,112},{16,0},{32,16},{48,32},{64,48},{80,64},{96,80},{112,96},{1... | collective-permute-start | bytes 4128776 | tf_op jit(solution)/shard_map/ppermute | solution.py:26
  144.0 16.0 %collective-permute-done.3 = bf16[128,5376]{1,0:T(8,128)(2,1)S(1)} collective-permute-done((bf16[128,5376]{1,0:T(8,128)(2,1)S(1)}, bf16[128,5376]{1,0:T(8,128)(2,1)S(1)}, u32[]{:S(2)}, u32[]{:S(2)}) %collective-permute-start.3) | collective-permute-done | bytes 1376288 | tf_op jit(solution)/shard_map/ppermute | solution.py:23
  160.0 1.1 copy-done.2
  161.1 3.0 %collective-permute-start.7 = (bf16[128,5376]{1,0:T(8,128)(2,1)}, bf16[128,5376]{1,0:T(8,128)(2,1)}, u32[]{:S(2)}, u32[]{:S(2)}) collective-permute-start(bf16[128,5376]{1,0:T(8,128)(2,1)} %collective-permute-done.6), channel_id=1, source_target_pairs={{0,112},{16,0},{32,16},{48,32},{64,48},{80,64},{96,80},{112,96},{1... | collective-permute-start | bytes 4128776 | tf_op jit(solution)/shard_map/ppermute | solution.py:26
  164.1 16.1 %collective-permute-done.4 = bf16[128,5376]{1,0:T(8,128)(2,1)} collective-permute-done((bf16[128,5376]{1,0:T(8,128)(2,1)S(1)}, bf16[128,5376]{1,0:T(8,128)(2,1)}, u32[]{:S(2)}, u32[]{:S(2)}) %collective-permute-start.4) | collective-permute-done | bytes 1376288 | tf_op jit(solution)/shard_map/ppermute | solution.py:23
  180.2 3.8 %constant_dynamic-slice_fusion.2 = (bf16[1024,896]{1,0:T(8,128)(2,1)S(1)}, bf16[1024,896]{1,0:T(8,128)(2,1)S(1)}, bf16[1024,896]{1,0:T(8,128)(2,1)S(1)}, bf16[1024,896]{1,0:T(8,128)(2,1)S(1)}) fusion(bf16[1024,1792]{1,0:T(8,128)(2,1)} %param.6, s32[]{:T(128)S(6)} %select_n.28, s32[]{:T(128)S(6)} %select_n.27, bf16[1024,1792]{1,0:T(8,128)(2,1)} %param.5), kind=kLoop, calls=%fused_computation.90 | loop fusion | bytes 14680072 | tf_op jit(solution)/shard_map/dynamic_slice | solution.py:8
  184.1 1.1 fusion.30
  185.1 2.9 %collective-permute-start.8 = (bf16[128,5376]{1,0:T(8,128)(2,1)}, bf16[128,5376]{1,0:T(8,128)(2,1)S(1)}, u32[]{:S(2)}, u32[]{:S(2)}) collective-permute-start(bf16[128,5376]{1,0:T(8,128)(2,1)} %collective-permute-done.7), channel_id=1, source_target_pairs={{0,112},{16,0},{32,16},{48,32},{64,48},{80,64},{96,80},{112,96},{1... | collective-permute-start | bytes 4128776 | tf_op jit(solution)/shard_map/ppermute | solution.py:26
  188.0 11.4 %collective-permute-done.5 = bf16[128,5376]{1,0:T(8,128)(2,1)} collective-permute-done((bf16[128,5376]{1,0:T(8,128)(2,1)}, bf16[128,5376]{1,0:T(8,128)(2,1)}, u32[]{:S(2)}, u32[]{:S(2)}) %collective-permute-start.5) | collective-permute-done | bytes 1376288 | tf_op jit(solution)/shard_map/ppermute | solution.py:23
  199.4 1.4 constant_dynamic-update-slice_fusion.20
  200.9 1.5 constant_dynamic-update-slice_fusion.19
  202.6 0.2 constant_dynamic-update-slice_fusion.28
  202.9 1.4 constant_dynamic-update-slice_fusion.15
  204.3 1.4 constant_dynamic-update-slice_fusion.14
  205.8 1.4 constant_dynamic-update-slice_fusion.12
  207.3 1.4 constant_dynamic-update-slice_fusion.11
  208.9 0.2 constant_dynamic-update-slice_fusion.24
  209.2 1.4 constant_dynamic-update-slice_fusion.7
  210.7 1.4 constant_dynamic-update-slice_fusion.6
  212.2 7.3 %copy-done.13 = bf16[2048,5376]{1,0:T(8,128)(2,1)} copy-done((bf16[2048,5376]{1,0:T(8,128)(2,1)}, bf16[2048,5376]{1,0:T(8,128)(2,1)S(1)}, u32[]{:S(2)}) %copy-start.13) | copy-done | bytes 22020120
  219.5 12.1 %fusion.9 = bf16[1024,1024]{1,0:T(8,128)(2,1)} fusion(bf16[1024,896]{1,0:T(8,128)(2,1)S(1)} %get-tuple-element.31, bf16[1024,896]{1,0:T(8,128)(2,1)S(1)} %get-tuple-element.38, bf16[1024,896]{1,0:T(8,128)(2,1)S(1)} %get-tuple-element.30, bf16[1024,896]{1,0:T(8,128)(2,1)S(1)} %get-tuple-element.39, bf16[2048,5376]{1,0:T(8,128)(2,1)} %copy-done.13, ...), kind=kOutput, calls=%fused_computation.14 | convolution fusion | flops 7546601472 | bytes 16777220 | tf_op jit(solution)/shard_map/dot_general | solution.py:90
  231.6 5.7 %all-to-all-start.2 = ((bf16[8,128,1024]{2,1,0:T(8,128)(2,1)}), bf16[8,128,1024]{2,1,0:T(8,128)(2,1)}, u32[]{:S(2)}, u32[]{:S(2)}) async-start(bf16[8,128,1024]{2,1,0:T(8,128)(2,1)} %bitcast.17), calls=%async_computation.3 | async-start | bytes 4194304 | tf_op jit(solution)/shard_map/all_to_all | solution.py:95
  237.3 4.7 %fusion.20 = bf16[1024,896]{1,0:T(8,128)(2,1)S(1)} fusion(bf16[1024,1024]{1,0:T(8,128)(2,1)} %bitcast.15, bf16[2048,5376]{1,0:T(8,128)(2,1)} %copy-done.13, s32[]{:T(128)S(6)} %select_n.30), kind=kOutput, calls=%fused_computation.21 | convolution fusion | flops 1879048192 | bytes 5767172 | tf_op jit(solution)/shard_map/dot_general | solution.py:99
  242.0 3.9 %fusion.16 = bf16[1024,896]{1,0:T(8,128)(2,1)S(1)} fusion(bf16[1024,1024]{1,0:T(8,128)(2,1)S(1)} %bitcast.16, bf16[2048,5376]{1,0:T(8,128)(2,1)} %copy-done.13, s32[]{:T(128)S(6)} %select_n.30, s32[]{:T(128)S(6)} %add.60), kind=kOutput, calls=%fused_computation.17 | convolution fusion | flops 1879048192 | bytes 5767176 | tf_op jit(solution)/shard_map/dot_general | solution.py:99
  245.9 5.2 %add_convert_fusion = bf16[1024,896]{1,0:T(8,128)(2,1)} fusion(bf16[1024,896]{1,0:T(8,128)(2,1)S(1)} %fusion.16, bf16[1024,1024]{1,0:T(8,128)(2,1)S(1)} %bitcast.11, bf16[2048,5376]{1,0:T(8,128)(2,1)} %copy-done.13, s32[]{:T(128)S(6)} %select_n.30, s32[]{:T(128)S(6)} %add.61), kind=kOutput, calls=%fused_computation.12 | convolution fusion | flops 1883635712 | bytes 7602184 | tf_op jit(solution)/shard_map/dot_general | solution.py:100
  251.1 5.2 %add_convert_fusion.1 = bf16[1024,896]{1,0:T(8,128)(2,1)} fusion(bf16[1024,896]{1,0:T(8,128)(2,1)S(1)} %fusion.20, bf16[1024,1024]{1,0:T(8,128)(2,1)S(1)} %bitcast.12, bf16[2048,5376]{1,0:T(8,128)(2,1)} %copy-done.13, s32[]{:T(128)S(6)} %select_n.30, s32[]{:T(128)S(6)} %add.59), kind=kOutput, calls=%fused_computation.13 | convolution fusion | flops 1883635712 | bytes 7602184 | tf_op jit(solution)/shard_map/dot_general | solution.py:100
  256.3 1.1 all-to-all-done.2
  257.4 2.7 %reduce_sum.12 = bf16[128,1024]{1,0:T(8,128)(2,1)} reduce(bf16[8,128,1024]{2,1,0:T(8,128)(2,1)} %all-to-all-done.2, bf16[]{:T(256)} %constant.49.clone.1), dimensions={0}, to_apply=%region_1.2 | reduce | flops 917504 | bytes 2359298 | tf_op jit(solution)/shard_map/reduce_sum | solution.py:96
  (57 shorter events, 1.1 us)
Async XLA Ops:
  7.2 99.1 %reduce-scatter.2.cloned.1.call-start = ((), (), s32[]{:S(2)}) async-start(), calls=%async_computation.4 | async-start | bytes 8257536 | tf_op jit(solution)/shard_map/reduce_scatter | solution.py:46
  7.2 32.0 %copy-start.8 = (bf16[1024,1792]{1,0:T(8,128)(2,1)S(1)}, bf16[1024,1792]{1,0:T(8,128)(2,1)}, u32[]{:S(2)}) copy-start(bf16[1024,1792]{1,0:T(8,128)(2,1)} %param.6) | copy-start | bytes 11010052
  39.2 5.4 %copy-start.10 = (bf16[8,128,1024]{2,1,0:T(8,128)(2,1)}, bf16[8,128,1024]{2,1,0:T(8,128)(2,1)S(1)}, u32[]{:S(2)}) copy-start(bf16[8,128,1024]{2,1,0:T(8,128)(2,1)S(1)} %all_to_all.23) | copy-start | bytes 6291460
  39.2 5.4 %copy-start.9 = (bf16[1024,1792]{1,0:T(8,128)(2,1)S(1)}, bf16[1024,1792]{1,0:T(8,128)(2,1)}, u32[]{:S(2)}) copy-start(bf16[1024,1792]{1,0:T(8,128)(2,1)} %param.5) | copy-start | bytes 11010052
  56.6 0.9 copy-start.15
  57.5 15.5 %copy-start.14 = (bf16[128,1792]{1,0:T(8,128)(2,1)S(1)}, bf16[128,1792]{1,0:T(8,128)(2,1)}, u32[]{:S(2)}) copy-start(bf16[128,1792]{1,0:T(8,128)(2,1)} %param.7) | copy-start | bytes 1376260
  57.6 8.1 %collective-permute-start = (bf16[128,1024]{1,0:T(8,128)(2,1)S(1)}, bf16[128,1024]{1,0:T(8,128)(2,1)S(1)}, u32[]{:S(2)}, u32[]{:S(2)}) collective-permute-start(bf16[128,1024]{1,0:T(8,128)(2,1)S(1)} %copy-done.15), channel_id=1, source_target_pairs={{0,1},{1,0},{2,3},{3,2},{4,5},{5,4},{6,7},{7,6},{8,9},{9,8},{10,11... | collective-permute-start | bytes 786440 | tf_op jit(solution)/shard_map/ppermute | solution.py:42
  67.3 28.4 %all-to-all-start.1 = ((bf16[8,128,1024]{2,1,0:T(8,128)(2,1)}), bf16[8,128,1024]{2,1,0:T(8,128)(2,1)S(1)}, u32[]{:S(2)}, u32[]{:S(2)}) async-start(bf16[8,128,1024]{2,1,0:T(8,128)(2,1)} %tile.5), calls=%async_computation.2 | async-start | bytes 4194304 | tf_op jit(solution)/shard_map/all_to_all | solution.py:40
  107.4 72.7 %copy-start.4 = (bf16[128,1792]{1,0:T(8,128)(2,1)}, bf16[128,1792]{1,0:T(8,128)(2,1)S(1)}, u32[]{:S(2)}) copy-start(bf16[128,1792]{1,0:T(8,128)(2,1)S(1)} %get-tuple-element.17) | copy-start | bytes 1376260
  107.5 72.7 %copy-start.6 = (bf16[128,1792]{1,0:T(8,128)(2,1)}, bf16[128,1792]{1,0:T(8,128)(2,1)S(1)}, u32[]{:S(2)}) copy-start(bf16[128,1792]{1,0:T(8,128)(2,1)S(1)} %get-tuple-element.16) | copy-start | bytes 1376260
  107.8 13.2 %collective-permute-start.1 = (bf16[128,1792]{1,0:T(8,128)(2,1)S(1)}, bf16[128,1792]{1,0:T(8,128)(2,1)S(1)}, u32[]{:S(2)}, u32[]{:S(2)}) collective-permute-start(bf16[128,1792]{1,0:T(8,128)(2,1)S(1)} %pad_maximum_fusion.1), channel_id=1, source_target_pairs={{0,1},{1,0},{2,3},{3,2},{4,5},{5,4},{6,7},{7,6},{8,9},{9,8},{10,11... | collective-permute-start | bytes 1376264 | tf_op jit(solution)/shard_map/ppermute | solution.py:73
  121.0 19.0 %collective-permute-start.2 = (bf16[128,5376]{1,0:T(8,128)(2,1)S(1)}, bf16[128,5376]{1,0:T(8,128)(2,1)S(1)}, u32[]{:S(2)}, u32[]{:S(2)}) collective-permute-start(bf16[128,5376]{1,0:T(8,128)(2,1)S(1)} %constant_dynamic-update-slice_fusion), channel_id=1, source_target_pairs={{0,16},{16,32},{32,48},{48,64},{64,80},{80,96},{96,112},{112,0},{1... | collective-permute-start | bytes 4128776 | tf_op jit(solution)/shard_map/ppermute | solution.py:23
  140.0 1.1 copy-start
  141.1 18.9 %collective-permute-start.3 = (bf16[128,5376]{1,0:T(8,128)(2,1)S(1)}, bf16[128,5376]{1,0:T(8,128)(2,1)S(1)}, u32[]{:S(2)}, u32[]{:S(2)}) collective-permute-start(bf16[128,5376]{1,0:T(8,128)(2,1)S(1)} %collective-permute-done.2), channel_id=1, source_target_pairs={{0,16},{16,32},{32,48},{48,64},{64,80},{80,96},{96,112},{112,0},{1... | collective-permute-start | bytes 4128776 | tf_op jit(solution)/shard_map/ppermute | solution.py:23
  141.1 20.0 %collective-permute-start.6 = (bf16[128,5376]{1,0:T(8,128)(2,1)S(1)}, bf16[128,5376]{1,0:T(8,128)(2,1)}, u32[]{:S(2)}, u32[]{:S(2)}) collective-permute-start(bf16[128,5376]{1,0:T(8,128)(2,1)S(1)} %constant_dynamic-update-slice_fusion), channel_id=1, source_target_pairs={{0,112},{16,0},{32,16},{48,32},{64,48},{80,64},{96,80},{112,96},{1... | collective-permute-start | bytes 4128776 | tf_op jit(solution)/shard_map/ppermute | solution.py:26
  160.0 1.1 copy-start.2
  161.1 19.1 %collective-permute-start.4 = (bf16[128,5376]{1,0:T(8,128)(2,1)S(1)}, bf16[128,5376]{1,0:T(8,128)(2,1)}, u32[]{:S(2)}, u32[]{:S(2)}) collective-permute-start(bf16[128,5376]{1,0:T(8,128)(2,1)S(1)} %collective-permute-done.3), channel_id=1, source_target_pairs={{0,16},{16,32},{32,48},{48,64},{64,80},{80,96},{96,112},{112,0},{1... | collective-permute-start | bytes 4128776 | tf_op jit(solution)/shard_map/ppermute | solution.py:23
  161.1 24.0 %collective-permute-start.7 = (bf16[128,5376]{1,0:T(8,128)(2,1)}, bf16[128,5376]{1,0:T(8,128)(2,1)}, u32[]{:S(2)}, u32[]{:S(2)}) collective-permute-start(bf16[128,5376]{1,0:T(8,128)(2,1)} %collective-permute-done.6), channel_id=1, source_target_pairs={{0,112},{16,0},{32,16},{48,32},{64,48},{80,64},{96,80},{112,96},{1... | collective-permute-start | bytes 4128776 | tf_op jit(solution)/shard_map/ppermute | solution.py:26
  180.2 19.3 %collective-permute-start.5 = (bf16[128,5376]{1,0:T(8,128)(2,1)}, bf16[128,5376]{1,0:T(8,128)(2,1)}, u32[]{:S(2)}, u32[]{:S(2)}) collective-permute-start(bf16[128,5376]{1,0:T(8,128)(2,1)} %collective-permute-done.4), channel_id=1, source_target_pairs={{0,16},{16,32},{32,48},{48,64},{64,80},{80,96},{96,112},{112,0},{1... | collective-permute-start | bytes 4128776 | tf_op jit(solution)/shard_map/ppermute | solution.py:23
  180.2 3.8 %copy-start.5 = (bf16[128,1792]{1,0:T(8,128)(2,1)S(1)}, bf16[128,1792]{1,0:T(8,128)(2,1)}, u32[]{:S(2)}) copy-start(bf16[128,1792]{1,0:T(8,128)(2,1)} %copy-done.4) | copy-start | bytes 1376260
  180.2 3.8 %copy-start.7 = (bf16[128,1792]{1,0:T(8,128)(2,1)S(1)}, bf16[128,1792]{1,0:T(8,128)(2,1)}, u32[]{:S(2)}) copy-start(bf16[128,1792]{1,0:T(8,128)(2,1)} %copy-done.6) | copy-start | bytes 1376260
  184.0 18.3 %copy-start.3 = (bf16[128,5376]{1,0:T(8,128)(2,1)S(1)}, bf16[128,5376]{1,0:T(8,128)(2,1)}, u32[]{:S(2)}) copy-start(bf16[128,5376]{1,0:T(8,128)(2,1)} %copy-done.2) | copy-start | bytes 4128772
  185.1 17.3 %copy-start.1 = (bf16[128,5376]{1,0:T(8,128)(2,1)S(1)}, bf16[128,5376]{1,0:T(8,128)(2,1)}, u32[]{:S(2)}) copy-start(bf16[128,5376]{1,0:T(8,128)(2,1)} %copy-done) | copy-start | bytes 4128772
  185.1 20.6 %collective-permute-start.8 = (bf16[128,5376]{1,0:T(8,128)(2,1)}, bf16[128,5376]{1,0:T(8,128)(2,1)S(1)}, u32[]{:S(2)}, u32[]{:S(2)}) collective-permute-start(bf16[128,5376]{1,0:T(8,128)(2,1)} %collective-permute-done.7), channel_id=1, source_target_pairs={{0,112},{16,0},{32,16},{48,32},{64,48},{80,64},{96,80},{112,96},{1... | collective-permute-start | bytes 4128776 | tf_op jit(solution)/shard_map/ppermute | solution.py:26
  200.8 1.7 copy-start.12
  212.2 7.3 %copy-start.13 = (bf16[2048,5376]{1,0:T(8,128)(2,1)}, bf16[2048,5376]{1,0:T(8,128)(2,1)S(1)}, u32[]{:S(2)}) copy-start(bf16[2048,5376]{1,0:T(8,128)(2,1)S(1)} %constant_dynamic-update-slice_fusion.5) | copy-start | bytes 66060292
  231.6 25.8 %all-to-all-start.2 = ((bf16[8,128,1024]{2,1,0:T(8,128)(2,1)}), bf16[8,128,1024]{2,1,0:T(8,128)(2,1)}, u32[]{:S(2)}, u32[]{:S(2)}) async-start(bf16[8,128,1024]{2,1,0:T(8,128)(2,1)} %bitcast.17), calls=%async_computation.3 | async-start | bytes 4194304 | tf_op jit(solution)/shard_map/all_to_all | solution.py:95
  237.3 4.7 %copy-start.11 = (bf16[8,128,1024]{2,1,0:T(8,128)(2,1)S(1)}, bf16[8,128,1024]{2,1,0:T(8,128)(2,1)}, u32[]{:S(2)}) copy-start(bf16[8,128,1024]{2,1,0:T(8,128)(2,1)} %copy-done.10) | copy-start | bytes 6291460
Sparse Core Ops, SparseCore 0:
  56.7 49.4 reduce-scatter.1
